TPU v7x, 32 devices: a whole 2x2x4 slice. The times are simulated.
32 devices in a mesh: groups: 2 (over y), ctx: 4 (over z), sub: 2 (over x), head: 2 (over core).
Axes of the slice: x: 2, y: 2, z: 4, core: 2. Of those that a mesh axis runs over, the one named last changes fastest.
Arguments:
- queries: bfloat16 [32, 10240, 128], P(('sub', 'head'), ('groups', 'ctx')), parts along dimension 1, may hold values from -6 to 6
- keys: bfloat16 [32, 10240, 128], P(('sub', 'head'), ('groups', 'ctx')), parts along dimension 1, may hold values from -6 to 6
- values: bfloat16 [32, 10240, 128], P(('sub', 'head'), ('groups', 'ctx')), parts along dimension 1, may hold values from -90 to 90
- out_grad: bfloat16 [32, 10240, 128], P(('sub', 'head'), ('groups', 'ctx')), parts along dimension 1, may hold values from -6 to 6
- norm_gain: float32 [32, 128], P(('sub', 'head')), may hold values from 0.25 to 1.75
- doc_ids: int32 [40], P(('groups', 'ctx')), parts along dimension 0, may hold values from 0 to 3, never falling along the last dimension, each value on 1 to 10 neighbouring positions
Outputs:
- grad_queries: bfloat16 [32, 10240, 128], P(('sub', 'head'), ('groups', 'ctx')), parts along dimension 1
- grad_keys: bfloat16 [32, 10240, 128], P(('sub', 'head'), ('groups', 'ctx')), parts along dimension 1
- grad_values: bfloat16 [32, 10240, 128], P(('sub', 'head'), ('groups', 'ctx')), parts along dimension 1
There are 2 independent parts, one for each index of `groups`. A program takes and returns all parts, laid end to end along the dimension named above; an argument that names none is the same for every part. Nothing has to cross between parts.
Inputs may be any that keep to these rules, and one draw needn't show every extreme that they name: `doc_ids`: never falls; each of its 4 values labels 1 to 10 consecutive blocks, one value exactly 10.
All inputs are finite; a program needn't handle non-finite values.
Results may differ from a plain program's by a relative error of at most 0.0058.
Values sent between devices are 32-bit elements; how exact they have to be, the bound alone decides.
No kernel may reach another device: no remote copies, remote signals or barrier semaphores. Data moves between devices by JAX's collectives and lax.ppermute only.
A program may use at most 128 MiB of HBM per device.

v0:
```python
import jax
import jax.numpy as jnp
from jax import lax
from jax.sharding import PartitionSpec as P


def segmented_scan(doc, state, axis, reverse):
    peers = lax.axis_size(axis)
    index = lax.axis_index(axis)
    none_doc = jnp.float32(-1.0)

    def shift(value, step):
        if reverse:
            pairs = [(j, j - step) for j in range(step, peers)]
        else:
            pairs = [(j, j + step) for j in range(peers - step)]
        return lax.ppermute(value, axis, pairs)

    def combine(near_doc, near_state, far_doc, far_state):
        joined = (near_doc == far_doc).astype(jnp.float32)
        return (near_doc, near_state + joined * far_state)

    if peers == 1:
        return (none_doc, jnp.zeros_like(state))
    got_doc, got_state = shift((doc, state), 1)
    valid = index >= 1 if not reverse else index <= peers - 2
    ex_doc = jnp.where(valid, got_doc, none_doc)
    ex_state = jnp.where(valid, got_state, 0.0)
    in_doc, in_state = combine(doc, state, ex_doc, ex_state)
    covered = 1
    while covered < peers - 1:
        step = covered + 1
        got_doc, got_state = shift((in_doc, in_state), step)
        valid = index >= step if not reverse else index <= peers - 1 - step
        got_doc = jnp.where(valid, got_doc, none_doc)
        got_state = jnp.where(valid, got_state, 0.0)
        ex_doc, ex_state = combine(ex_doc, ex_state, got_doc, got_state)
        covered = covered + step
        if covered < peers - 1:
            in_doc, in_state = combine(in_doc, in_state, got_doc, got_state)
    return (ex_doc, ex_state)


def on_device(queries, keys, values, out_grad, norm_gain, doc_ids):
    head_count, tok_count, head_width = queries.shape
    block_count = doc_ids.shape[0]
    block_len = tok_count // block_count
    block_shape = (head_count, block_count, block_len, head_width)
    highest_precision = lax.Precision.HIGHEST
    query_blocks = queries.reshape(block_shape)
    key_blocks = keys.reshape(block_shape)
    value_blocks = values.reshape(block_shape)
    row_ids = lax.broadcasted_iota(jnp.int32, (block_len, block_len), 0)
    col_ids = lax.broadcasted_iota(jnp.int32, (block_len, block_len), 1)
    causal = row_ids >= col_ids
    doc_values = doc_ids.astype(jnp.float32)
    block_pos = jnp.arange(block_count, dtype=jnp.int32)
    same_doc = doc_values[:, None] == doc_values[None, :]
    earlier_mask = (same_doc & (block_pos[None, :] < block_pos[:, None])).astype(jnp.float32)
    later_mask = (same_doc & (block_pos[None, :] > block_pos[:, None])).astype(jnp.float32)
    key_value_block = jnp.einsum(
        "hnid,hnie->hnde", key_blocks, value_blocks, preferred_element_type=jnp.float32
    )
    last_match = (doc_values == doc_values[-1]).astype(jnp.float32)
    device_kv = jnp.einsum("c,hcde->hde", last_match, key_value_block, precision=highest_precision)
    prior_doc, prior_state = segmented_scan(doc_values[-1], device_kv, "ctx", False)
    scores = jnp.einsum(
        "hnid,hnjd->hnij", query_blocks, key_blocks, preferred_element_type=jnp.float32
    )
    block_probs = jnp.where(causal, scores, 0.0).astype(jnp.bfloat16)
    intra_part = jnp.einsum(
        "hnij,hnjd->hnid", block_probs, value_blocks, preferred_element_type=jnp.float32
    )
    local_prefix = jnp.einsum(
        "bc,hcde->hbde", earlier_mask, key_value_block, precision=highest_precision
    )
    prior_match = (doc_values == prior_doc).astype(jnp.float32)
    entering = prior_match[None, :, None, None] * prior_state[:, None, :, :]
    preceding_states = (local_prefix + entering).astype(jnp.bfloat16)
    cross_block_part = jnp.einsum(
        "hnid,hnde->hnie", query_blocks, preceding_states, preferred_element_type=jnp.float32
    )
    raw_attn = (intra_part + cross_block_part).reshape(head_count, tok_count, head_width)
    feature_count = head_count * head_width * lax.axis_size(("sub", "head"))
    scaled = norm_gain[:, None, :] * out_grad.astype(jnp.float32)
    local_sums = jnp.stack(
        [jnp.sum(raw_attn * raw_attn, axis=(0, 2)), jnp.sum(scaled * raw_attn, axis=(0, 2))]
    )
    total_sums = lax.psum(local_sums, ("sub", "head"))
    root_mean = jnp.sqrt(total_sums[0] / feature_count + 1e-06)
    inner_mean = total_sums[1] / feature_count
    factor = inner_mean / (root_mean * root_mean)
    d_attn = ((scaled - raw_attn * factor[None, :, None]) / root_mean[None, :, None]).astype(
        jnp.bfloat16
    )
    output_grad_blocks = d_attn.reshape(block_shape)
    query_grad_block = jnp.einsum(
        "hnid,hnie->hnde", query_blocks, output_grad_blocks, preferred_element_type=jnp.float32
    )
    first_match = (doc_values == doc_values[0]).astype(jnp.float32)
    device_qd = jnp.einsum(
        "c,hcde->hde", first_match, query_grad_block, precision=highest_precision
    )
    next_doc, next_state = segmented_scan(doc_values[0], device_qd, "ctx", True)
    grad_scores = jnp.einsum(
        "hnid,hnjd->hnij", output_grad_blocks, value_blocks, preferred_element_type=jnp.float32
    )
    grad_probs = jnp.where(causal, grad_scores, 0.0).astype(jnp.bfloat16)
    query_gradient = jnp.einsum(
        "hnij,hnjd->hnid", grad_probs, key_blocks, preferred_element_type=jnp.float32
    )
    key_gradient = jnp.einsum(
        "hnij,hnid->hnjd", grad_probs, query_blocks, preferred_element_type=jnp.float32
    )
    value_gradient = jnp.einsum(
        "hnij,hnid->hnjd", block_probs, output_grad_blocks, preferred_element_type=jnp.float32
    )
    local_suffix = jnp.einsum(
        "bc,hcde->hbde", later_mask, query_grad_block, precision=highest_precision
    )
    next_match = (doc_values == next_doc).astype(jnp.float32)
    leaving = next_match[None, :, None, None] * next_state[:, None, :, :]
    following_states = (local_suffix + leaving).astype(jnp.bfloat16)
    query_gradient = query_gradient + jnp.einsum(
        "hnie,hnde->hnid", output_grad_blocks, preceding_states, preferred_element_type=jnp.float32
    )
    key_gradient = key_gradient + jnp.einsum(
        "hnie,hnde->hnid", value_blocks, following_states, preferred_element_type=jnp.float32
    )
    value_gradient = value_gradient + jnp.einsum(
        "hnid,hnde->hnie", key_blocks, following_states, preferred_element_type=jnp.float32
    )
    out_shape = (head_count, tok_count, head_width)
    return (
        query_gradient.reshape(out_shape).astype(jnp.bfloat16),
        key_gradient.reshape(out_shape).astype(jnp.bfloat16),
        value_gradient.reshape(out_shape).astype(jnp.bfloat16),
    )


def solution(mesh):
    return jax.shard_map(
        on_device,
        mesh=mesh,
        in_specs=(
            P(("sub", "head"), ("groups", "ctx"), None),
            P(("sub", "head"), ("groups", "ctx"), None),
            P(("sub", "head"), ("groups", "ctx"), None),
            P(("sub", "head"), ("groups", "ctx"), None),
            P(("sub", "head"), None),
            P(("groups", "ctx")),
        ),
        out_specs=(
            P(("sub", "head"), ("groups", "ctx"), None),
            P(("sub", "head"), ("groups", "ctx"), None),
            P(("sub", "head"), ("groups", "ctx"), None),
        ),
        check_vma=False,
    )
```

profile of v0, /device:TPU:0, one launch (start us, length us, event | category | flops | bytes accessed | tf_op | source)
XLA Modules:
  0.0 159.0 jit_solution(8993034932632156992)
XLA Ops:
  0.6 0.0 copy-start
  0.6 0.8 convert_element_type.63
  1.5 0.6 fusion.34
  2.0 1.3 collective-permute-start.6
  3.3 1.3 collective-permute-start.4
  4.6 7.6 %collective-permute-start.2 = (f32[]{:T(128)}, f32[]{:T(128)}, u32[]{:S(2)}, u32[]{:S(2)}) collective-permute-start(f32[]{:T(128)} %bitcast.7), channel_id=1, source_target_pairs={{0,8},{4,12},{1,9},{5,13},{2,10},{6,14},{3,11},{7,15},{16,24},{20,... | collective-permute-start | bytes 20 | tf_op jit(solution)/shard_map/ppermute | solution.py:17
  12.2 5.0 %collective-permute-start = (f32[]{:T(128)}, f32[]{:T(128)}, u32[]{:S(2)}, u32[]{:S(2)}) collective-permute-start(f32[]{:T(128)} %bitcast.7), channel_id=1, source_target_pairs={{0,4},{4,8},{8,12},{1,5},{5,9},{9,13},{2,6},{6,10},{10,14},{3,7},{... | collective-permute-start | bytes 20 | tf_op jit(solution)/shard_map/ppermute | solution.py:17
  17.2 3.4 %fusion.36 = f32[8,5,128,128]{3,2,1,0:T(8,128)S(1)} fusion(bf16[8,5,256,128]{3,2,1,0:T(8,128)(2,1)} %bitcast.105, bf16[8,5,256,128]{3,2,1,0:T(8,128)(2,1)} %bitcast.109), kind=kOutput, calls=%fused_computation.62 | convolution fusion | flops 335544320 | bytes 7864320 | tf_op jit(solution)/shard_map/hnid,hnie->hnde/dot_general | solution.py:61
  20.6 0.0 copy-start.2
  20.6 1.5 copy-done.2
  22.1 4.9 %fusion.6 = f32[1,8,128,128]{3,0,2,1:T(1,128)} fusion(f32[8,5,128,128]{3,2,1,0:T(8,128)S(1)} %fusion.36, f32[]{:T(128)} %bitcast.7, s32[5]{0:T(128)S(1)} %copy-done.16), kind=kOutput, calls=%fused_computation.16 | convolution fusion | flops 7864330 | bytes 3145752 | tf_op jit(solution)/shard_map/c,hcde->hde/dot_general | solution.py:65
  27.0 1.4 collective-permute-start.1
  28.5 0.0 copy-start.9
  28.5 3.4 %select_convert_fusion.1 = bf16[8,5,256,256]{3,2,1,0:T(8,128)(2,1)S(1)} fusion(pred[256,256]{1,0:T(8,128)(4,1)S(1)} %iota_compare_fusion, bf16[8,5,256,128]{3,2,1,0:T(8,128)(2,1)S(1)} %bitcast.95, bf16[8,5,256,128]{3,2,1,0:T(8,128)(2,1)} %bitcast.106), kind=kOutput, calls=%fused_computation.1 | convolution fusion | flops 676331520 | bytes 10551296 | tf_op jit(solution)/shard_map/hnid,hnjd->hnij/dot_general | solution.py:67
  31.9 4.0 %fusion.35 = f32[8,5,256,128]{3,2,1,0:T(8,128)} fusion(bf16[8,5,256,256]{3,2,1,0:T(8,128)(2,1)S(1)} %select_convert_fusion.1, bf16[8,5,256,128]{3,2,1,0:T(8,128)(2,1)S(1)} %bitcast.110), kind=kOutput, calls=%fused_computation.61 | convolution fusion | flops 671088640 | bytes 13107200 | tf_op jit(solution)/shard_map/hnij,hnjd->hnid/dot_general | solution.py:71
  35.9 0.0 collective-permute-done
  37.2 2.1 %collective-permute-done.1 = f32[8,128,128]{2,1,0:T(8,128)S(1)} collective-permute-done((f32[8,128,128]{2,1,0:T(8,128)}, f32[8,128,128]{2,1,0:T(8,128)S(1)}, u32[]{:S(2)}, u32[]{:S(2)}) %collective-permute-start.1) | collective-permute-done | bytes 524320 | tf_op jit(solution)/shard_map/ppermute | solution.py:17
  39.3 1.9 %multiply_add_fusion.3 = f32[8,128,128]{2,1,0:T(8,128)} fusion(f32[8,128,128]{2,1,0:T(8,128)} %bitcast.11, f32[8,128,128]{2,1,0:T(8,128)S(1)} %collective-permute-done.1, f32[]{:T(128)S(6)} %convert_element_type.66, pred[]{:T(512)S(6)} %ge.12), kind=kLoop, calls=%fused_computation.28 | loop fusion | flops 393216 | bytes 1572869 | tf_op jit(solution)/shard_map/add | solution.py:21
  41.2 4.8 %collective-permute-start.3 = (f32[8,128,128]{2,1,0:T(8,128)}, f32[8,128,128]{2,1,0:T(8,128)}, u32[]{:S(2)}, u32[]{:S(2)}) collective-permute-start(f32[8,128,128]{2,1,0:T(8,128)} %multiply_add_fusion.3), channel_id=1, source_target_pairs={{0,8},{4,12},{1,9},{5,13},{2,10},{6,14},{3,11},{7,15},{16,24},{20,... | collective-permute-start | bytes 1572872 | tf_op jit(solution)/shard_map/ppermute | solution.py:17
  46.0 7.2 %fusion.8 = f32[8,128,128,5]{2,3,1,0:T(8,128)} fusion(f32[8,5,128,128]{3,2,1,0:T(8,128)} %copy-done.2, f32[5]{0:T(128)S(1)} %convert_element_type.63), kind=kOutput, calls=%fused_computation.18 | convolution fusion | flops 39321676 | bytes 5242900 | tf_op jit(solution)/shard_map/bc,hcde->hbde/dot_general | solution.py:74
  53.2 0.0 collective-permute-done.4
  54.4 0.0 collective-permute-done.6
  55.1 0.0 collective-permute-done.2
  55.7 0.0 collective-permute-done.3
  55.7 0.1 multiply_add_fusion.2
  55.8 3.0 %fusion.11 = bf16[8,5,128,128]{3,2,1,0:T(8,128)(2,1)S(1)} fusion(f32[8,128,128,5]{2,3,1,0:T(8,128)} %fusion.8, f32[8,128,128]{2,1,0:T(8,128)S(1)} %multiply_add_fusion.2, f32[5]{0:T(128)S(1)} %get-tuple-element.6), kind=kLoop, calls=%fused_computation.23 | loop fusion | flops 1966080 | bytes 4456468 | tf_op jit(solution)/shard_map/convert_element_type | solution.py:79
  58.8 0.8 copy-done.7
  59.5 1.2 multiply_reduce_fusion
  60.7 0.0 copy-start.1
  60.8 1.1 copy-done.14
  61.9 0.8 fusion.2
  62.6 0.4 copy-done.1
  63.1 10.3 %psum.7 = f32[2,1280]{1,0:T(2,128)S(1)} all-reduce(f32[2,1280]{1,0:T(2,128)S(1)} %pad_maximum_fusion), channel_id=1, replica_groups=mesh['groups'=2,'ctx'=4,'sub'=2,'head'=2] {'sub','head'}, use_global_device_ids=true, to_apply=%region_2.3 | all-reduce | flops 2560 | bytes 20480 | tf_op jit(solution)/shard_map/psum | solution.py:89
  73.5 4.0 %fusion.5 = bf16[8,1280,128]{2,1,0:T(8,128)(2,1)S(1)} fusion(f32[8,5,256,128]{3,2,1,0:T(8,128)} %copy-done.1, bf16[8,1280,128]{2,1,0:T(8,128)(2,1)} %param.9, f32[1280]{0:T(1024)S(1)} %get-tuple-element.4, f32[1280]{0:T(1024)S(1)} %multiply_divide_fusion, f32[8,128]{1,0:T(8,128)S(1)} %copy-done.15), kind=kLoop, calls=%fused_computation.11 | loop fusion | flops 7864320 | bytes 10500096 | tf_op jit(solution)/shard_map/convert_element_type | solution.py:93
  77.5 0.0 copy-start.3
  77.5 7.4 %fusion.39 = f32[8,5,256,128]{3,2,1,0:T(8,128)} fusion(bf16[8,5,256,256]{3,2,1,0:T(8,128)(2,1)} %copy-done.6, bf16[8,5,256,128]{3,2,1,0:T(8,128)(2,1)S(1)} %bitcast.99), kind=kOutput, calls=%fused_computation.65 | convolution fusion | flops 671088640 | bytes 13107200 | tf_op jit(solution)/shard_map/hnij,hnid->hnjd/dot_general | solution.py:115
  84.9 2.4 %convolution_bitcast_fusion = f32[8,5,128,128]{2,3,1,0:T(8,128)} fusion(bf16[8,5,256,128]{3,2,1,0:T(8,128)(2,1)S(1)} %bitcast.100, bf16[8,5,256,128]{3,2,1,0:T(8,128)(2,1)S(1)} %bitcast.98), kind=kOutput, calls=%fused_computation.24 | convolution fusion | flops 335544320 | bytes 7864320 | tf_op jit(solution)/shard_map/hnid,hnie->hnde/dot_general | solution.py:97
  87.3 0.0 copy-done.3
  87.3 3.9 %select_convert_fusion = bf16[8,5,256,256]{3,2,1,0:T(8,128)(2,1)} fusion(pred[256,256]{1,0:T(8,128)(4,1)S(1)} %iota_compare_fusion, bf16[8,5,256,128]{3,2,1,0:T(8,128)(2,1)S(1)} %bitcast.101, bf16[8,5,256,128]{3,2,1,0:T(8,128)(2,1)S(1)} %bitcast.111), kind=kOutput, calls=%fused_computation | convolution fusion | flops 676331520 | bytes 10551296 | tf_op jit(solution)/shard_map/hnid,hnjd->hnij/dot_general | solution.py:105
  91.2 4.7 %copy.29 = f32[8,5,128,128]{3,1,2,0:T(8,128)} copy(f32[8,5,128,128]{2,3,1,0:T(8,128)} %convolution_bitcast_fusion) | data formatting | bytes 5242880 | tf_op jit(solution)/shard_map/hnid,hnie->hnde/dot_general | solution.py:97
  95.9 5.2 %fusion.25 = f32[1,8,128,128]{3,0,2,1:T(1,128)S(1)} fusion(f32[8,5,128,128]{3,1,2,0:T(8,128)} %copy.29, f32[]{:T(128)} %bitcast.21, s32[5]{0:T(128)S(1)} %copy-done.16), kind=kOutput, calls=%fused_computation.49 | convolution fusion | flops 7864330 | bytes 3145752 | tf_op jit(solution)/shard_map/c,hcde->hde/dot_general | solution.py:101
  101.1 0.0 slice-start.1
  101.1 1.4 collective-permute-start.5
  102.5 0.0 copy-start.8
  102.5 4.2 %fusion.38 = f32[8,5,256,128]{3,2,1,0:T(8,128)S(1)} fusion(bf16[8,5,256,256]{3,2,1,0:T(8,128)(2,1)} %select_convert_fusion, bf16[8,5,256,128]{3,2,1,0:T(8,128)(2,1)S(1)} %bitcast.97), kind=kOutput, calls=%fused_computation.64 | convolution fusion | flops 671088640 | bytes 13107200 | tf_op jit(solution)/shard_map/hnij,hnid->hnjd/dot_general | solution.py:112
  106.8 0.0 copy-start.5
  106.8 1.5 fusion.37
  108.3 17.3 %collective-permute-done.5 = f32[8,128,128]{2,1,0:T(8,128)S(1)} collective-permute-done((f32[8,128,128]{2,1,0:T(8,128)S(1)}, f32[8,128,128]{2,1,0:T(8,128)S(1)}, u32[]{:S(2)}, u32[]{:S(2)}) %collective-permute-start.5) | collective-permute-done | bytes 524320 | tf_op jit(solution)/shard_map/ppermute | solution.py:17
  125.6 0.1 multiply_add_fusion.1
  125.6 0.0 copy-start.4
  125.6 0.0 copy-start.13
  125.6 1.8 %collective-permute-start.7 = (f32[8,128,128]{2,1,0:T(8,128)S(1)}, f32[8,128,128]{2,1,0:T(8,128)S(1)}, u32[]{:S(2)}, u32[]{:S(2)}) collective-permute-start(f32[8,128,128]{2,1,0:T(8,128)S(1)} %multiply_add_fusion.1), channel_id=1, source_target_pairs={{8,0},{12,4},{9,1},{13,5},{10,2},{14,6},{11,3},{15,7},{24,16},{28,... | collective-permute-start | bytes 1572872 | tf_op jit(solution)/shard_map/ppermute | solution.py:17
  127.5 0.0 slice-start.2
  127.5 2.2 %fusion.19 = f32[8,128,128,5]{2,3,1,0:T(8,128)S(1)} fusion(f32[8,5,128,128]{3,1,2,0:T(8,128)S(1)} %copy-done.5, f32[5]{0:T(128)S(1)} %convert_element_type.63), kind=kOutput, calls=%fused_computation.44 | convolution fusion | flops 39321676 | bytes 5242900 | tf_op jit(solution)/shard_map/bc,hcde->hbde/dot_general | solution.py:118
  129.7 0.0 copy-done.4
  129.7 0.0 copy-done.13
  129.7 0.0 slice-start.3
  129.7 2.4 %add_convert_fusion = bf16[8,5,256,128]{3,2,1,0:T(8,128)(2,1)} fusion(f32[8,5,256,128]{3,2,1,0:T(8,128)S(1)} %fusion.37, bf16[8,5,256,128]{3,2,1,0:T(8,128)(2,1)S(1)} %bitcast.102, bf16[8,5,128,128]{3,2,1,0:T(8,128)(2,1)S(1)} %copy-done.13), kind=kOutput, calls=%fused_computation.13 | convolution fusion | flops 338165760 | bytes 11796480 | tf_op jit(solution)/shard_map/hnie,hnde->hnid/dot_general | solution.py:124
  132.2 21.3 %collective-permute-done.7 = f32[8,128,128]{2,1,0:T(8,128)S(1)} collective-permute-done((f32[8,128,128]{2,1,0:T(8,128)S(1)}, f32[8,128,128]{2,1,0:T(8,128)S(1)}, u32[]{:S(2)}, u32[]{:S(2)}) %collective-permute-start.7) | collective-permute-done | bytes 524320 | tf_op jit(solution)/shard_map/ppermute | solution.py:17
  153.4 0.1 multiply_add_fusion
  153.5 0.6 fusion.10
  154.2 0.0 copy-start.11
  154.2 2.4 %fusion = bf16[8,5,256,128]{3,2,1,0:T(8,128)(2,1)} fusion(f32[8,5,256,128]{3,2,1,0:T(8,128)S(1)} %bitcast.114, bf16[8,5,256,128]{3,2,1,0:T(8,128)(2,1)S(1)} %bitcast.108, bf16[8,5,128,128]{3,2,1,0:T(8,128)(2,1)S(1)} %fusion.10), kind=kOutput, calls=%fused_computation.3 | convolution fusion | flops 338165760 | bytes 11796480 | tf_op jit(solution)/shard_map/hnid,hnde->hnie/dot_general | solution.py:130
  156.6 2.4 %fusion.1 = bf16[8,5,256,128]{3,2,1,0:T(8,128)(2,1)} fusion(f32[8,5,256,128]{3,2,1,0:T(8,128)S(1)} %fusion.38, bf16[8,5,128,128]{3,2,1,0:T(8,128)(2,1)S(1)} %fusion.10, bf16[8,5,256,128]{3,2,1,0:T(8,128)(2,1)S(1)} %bitcast.112), kind=kOutput, calls=%fused_computation.5 | convolution fusion | flops 338165760 | bytes 11796480 | tf_op jit(solution)/shard_map/hnie,hnde->hnid/dot_general | solution.py:127
  (31 shorter events, 0.2 us)
Async XLA Ops:
  0.6 27.8 %copy-start = (bf16[8,1280,128]{2,1,0:T(8,128)(2,1)S(1)}, bf16[8,1280,128]{2,1,0:T(8,128)(2,1)}, u32[]{:S(2)}) copy-start(bf16[8,1280,128]{2,1,0:T(8,128)(2,1)} %param.6) | copy-start | bytes 7864324
  2.0 52.4 %collective-permute-start.6 = (f32[]{:T(128)}, f32[]{:T(128)}, u32[]{:S(2)}, u32[]{:S(2)}) collective-permute-start(f32[]{:T(128)} %bitcast.21), channel_id=1, source_target_pairs={{8,0},{12,4},{9,1},{13,5},{10,2},{14,6},{11,3},{15,7},{24,16},{28,... | collective-permute-start | bytes 20 | tf_op jit(solution)/shard_map/ppermute | solution.py:17
  3.3 49.9 %collective-permute-start.4 = (f32[]{:T(128)}, f32[]{:T(128)}, u32[]{:S(2)}, u32[]{:S(2)}) collective-permute-start(f32[]{:T(128)} %bitcast.21), channel_id=1, source_target_pairs={{4,0},{8,4},{12,8},{5,1},{9,5},{13,9},{6,2},{10,6},{14,10},{7,3},{... | collective-permute-start | bytes 20 | tf_op jit(solution)/shard_map/ppermute | solution.py:17
  4.6 50.5 %collective-permute-start.2 = (f32[]{:T(128)}, f32[]{:T(128)}, u32[]{:S(2)}, u32[]{:S(2)}) collective-permute-start(f32[]{:T(128)} %bitcast.7), channel_id=1, source_target_pairs={{0,8},{4,12},{1,9},{5,13},{2,10},{6,14},{3,11},{7,15},{16,24},{20,... | collective-permute-start | bytes 20 | tf_op jit(solution)/shard_map/ppermute | solution.py:17
  12.2 23.7 %collective-permute-start = (f32[]{:T(128)}, f32[]{:T(128)}, u32[]{:S(2)}, u32[]{:S(2)}) collective-permute-start(f32[]{:T(128)} %bitcast.7), channel_id=1, source_target_pairs={{0,4},{4,8},{8,12},{1,5},{5,9},{9,13},{2,6},{6,10},{10,14},{3,7},{... | collective-permute-start | bytes 20 | tf_op jit(solution)/shard_map/ppermute | solution.py:17
  17.2 4.9 %copy-start.16 = (s32[5]{0:T(128)S(1)}, s32[5]{0:T(128)}, u32[]{:S(2)}) copy-start(s32[5]{0:T(128)} %param.11) | copy-start | bytes 64
  20.6 1.5 copy-start.2
  27.0 12.3 %collective-permute-start.1 = (f32[8,128,128]{2,1,0:T(8,128)}, f32[8,128,128]{2,1,0:T(8,128)S(1)}, u32[]{:S(2)}, u32[]{:S(2)}) collective-permute-start(f32[8,128,128]{2,1,0:T(8,128)} %bitcast.11), channel_id=1, source_target_pairs={{0,4},{4,8},{8,12},{1,5},{5,9},{9,13},{2,6},{6,10},{10,14},{3,7},{... | collective-permute-start | bytes 1572872 | tf_op jit(solution)/shard_map/ppermute | solution.py:17
  28.5 3.4 %copy-start.9 = (bf16[8,1280,128]{2,1,0:T(8,128)(2,1)S(1)}, bf16[8,1280,128]{2,1,0:T(8,128)(2,1)}, u32[]{:S(2)}) copy-start(bf16[8,1280,128]{2,1,0:T(8,128)(2,1)} %param.8) | copy-start | bytes 7864324
  31.9 4.0 %copy-start.6 = (bf16[8,5,256,256]{3,2,1,0:T(8,128)(2,1)}, bf16[8,5,256,256]{3,2,1,0:T(8,128)(2,1)S(1)}, u32[]{:S(2)}) copy-start(bf16[8,5,256,256]{3,2,1,0:T(8,128)(2,1)S(1)} %select_convert_fusion.1) | copy-start | bytes 15728644
  41.2 14.5 %collective-permute-start.3 = (f32[8,128,128]{2,1,0:T(8,128)}, f32[8,128,128]{2,1,0:T(8,128)}, u32[]{:S(2)}, u32[]{:S(2)}) collective-permute-start(f32[8,128,128]{2,1,0:T(8,128)} %multiply_add_fusion.3), channel_id=1, source_target_pairs={{0,8},{4,12},{1,9},{5,13},{2,10},{6,14},{3,11},{7,15},{16,24},{20,... | collective-permute-start | bytes 1572872 | tf_op jit(solution)/shard_map/ppermute | solution.py:17
  55.8 3.7 %copy-start.7 = (f32[8,5,256,128]{3,2,1,0:T(8,128)S(1)}, f32[8,5,256,128]{3,2,1,0:T(8,128)}, u32[]{:S(2)}) copy-start(f32[8,5,256,128]{3,2,1,0:T(8,128)} %fusion.35) | copy-start | bytes 15728644
  59.5 1.2 copy-start.12
  59.5 2.3 %copy-start.14 = (bf16[8,1280,128]{2,1,0:T(8,128)(2,1)S(1)}, bf16[8,1280,128]{2,1,0:T(8,128)(2,1)}, u32[]{:S(2)}) copy-start(bf16[8,1280,128]{2,1,0:T(8,128)(2,1)} %param.9) | copy-start | bytes 7864324
  59.5 2.3 %copy-start.15 = (f32[8,128]{1,0:T(8,128)S(1)}, f32[8,128]{1,0:T(8,128)}, u32[]{:S(2)}) copy-start(f32[8,128]{1,0:T(8,128)} %param.10) | copy-start | bytes 12292
  60.7 2.4 %copy-start.1 = (f32[8,5,256,128]{3,2,1,0:T(8,128)}, f32[8,5,256,128]{3,2,1,0:T(8,128)S(1)}, u32[]{:S(2)}) copy-start(f32[8,5,256,128]{3,2,1,0:T(8,128)S(1)} %get-tuple-element.10) | copy-start | bytes 15728644
  77.5 9.8 %copy-start.3 = (bf16[8,1280,128]{2,1,0:T(8,128)(2,1)}, bf16[8,1280,128]{2,1,0:T(8,128)(2,1)S(1)}, u32[]{:S(2)}) copy-start(bf16[8,1280,128]{2,1,0:T(8,128)(2,1)S(1)} %fusion.5) | copy-start | bytes 7864324
  84.9 2.4 %copy-start.10 = (bf16[8,1280,128]{2,1,0:T(8,128)(2,1)S(1)}, bf16[8,1280,128]{2,1,0:T(8,128)(2,1)}, u32[]{:S(2)}) copy-start(bf16[8,1280,128]{2,1,0:T(8,128)(2,1)} %param.8) | copy-start | bytes 7864324
  95.9 10.9 %slice-start = ((s8[5242880]{0:T(1024)(128)(4,1)}), s8[4194304]{0:T(1024)(128)(4,1)S(1)}, s32[]{:S(2)}) async-start(s8[5242880]{0:T(1024)(128)(4,1)} %bitcast.103), calls=%async_computation | async-start | bytes 8388608
  101.1 5.7 %slice-start.1 = ((s8[5242880]{0:T(1024)(128)(4,1)}), s8[1048576]{0:T(1024)(128)(4,1)S(1)}, s32[]{:S(2)}) async-start(s8[5242880]{0:T(1024)(128)(4,1)} %bitcast.103), calls=%async_computation.1 | async-start | bytes 2097152
  101.1 24.5 %collective-permute-start.5 = (f32[8,128,128]{2,1,0:T(8,128)S(1)}, f32[8,128,128]{2,1,0:T(8,128)S(1)}, u32[]{:S(2)}, u32[]{:S(2)}) collective-permute-start(f32[8,128,128]{2,1,0:T(8,128)S(1)} %bitcast.118), channel_id=1, source_target_pairs={{4,0},{8,4},{12,8},{5,1},{9,5},{13,9},{6,2},{10,6},{14,10},{7,3},{... | collective-permute-start | bytes 1572872 | tf_op jit(solution)/shard_map/ppermute | solution.py:17
  102.5 4.2 %copy-start.8 = (bf16[8,1280,128]{2,1,0:T(8,128)(2,1)S(1)}, bf16[8,1280,128]{2,1,0:T(8,128)(2,1)}, u32[]{:S(2)}) copy-start(bf16[8,1280,128]{2,1,0:T(8,128)(2,1)} %param.7) | copy-start | bytes 7864324
  106.8 20.7 %copy-start.5 = (f32[8,5,128,128]{3,1,2,0:T(8,128)S(1)}, f32[8,5,128,128]{3,1,2,0:T(8,128)}, u32[]{:S(2)}) copy-start(f32[8,5,128,128]{3,1,2,0:T(8,128)} %copy.29) | copy-start | bytes 7864324
  125.6 4.1 %copy-start.4 = (bf16[8,1280,128]{2,1,0:T(8,128)(2,1)S(1)}, bf16[8,1280,128]{2,1,0:T(8,128)(2,1)}, u32[]{:S(2)}) copy-start(bf16[8,1280,128]{2,1,0:T(8,128)(2,1)} %copy-done.3) | copy-start | bytes 7864324
  125.6 4.1 %copy-start.13 = (bf16[8,5,128,128]{3,2,1,0:T(8,128)(2,1)S(1)}, bf16[8,5,128,128]{3,2,1,0:T(8,128)(2,1)}, u32[]{:S(2)}) copy-start(bf16[8,5,128,128]{3,2,1,0:T(8,128)(2,1)} %copy-done.12) | copy-start | bytes 3932164
  125.6 27.8 %collective-permute-start.7 = (f32[8,128,128]{2,1,0:T(8,128)S(1)}, f32[8,128,128]{2,1,0:T(8,128)S(1)}, u32[]{:S(2)}, u32[]{:S(2)}) collective-permute-start(f32[8,128,128]{2,1,0:T(8,128)S(1)} %multiply_add_fusion.1), channel_id=1, source_target_pairs={{8,0},{12,4},{9,1},{13,5},{10,2},{14,6},{11,3},{15,7},{24,16},{28,... | collective-permute-start | bytes 1572872 | tf_op jit(solution)/shard_map/ppermute | solution.py:17
  127.5 26.7 %slice-start.2 = ((s8[5242880]{0:T(1024)(128)(4,1)}), s8[4194304]{0:T(1024)(128)(4,1)S(1)}, s32[]{:S(2)}) async-start(s8[5242880]{0:T(1024)(128)(4,1)} %bitcast.113), calls=%async_computation.2 | async-start | bytes 8388608
  129.7 24.5 %slice-start.3 = ((s8[5242880]{0:T(1024)(128)(4,1)}), s8[1048576]{0:T(1024)(128)(4,1)S(1)}, s32[]{:S(2)}) async-start(s8[5242880]{0:T(1024)(128)(4,1)} %bitcast.113), calls=%async_computation.3 | async-start | bytes 2097152
  154.2 2.4 %copy-start.11 = (bf16[8,1280,128]{2,1,0:T(8,128)(2,1)S(1)}, bf16[8,1280,128]{2,1,0:T(8,128)(2,1)}, u32[]{:S(2)}) copy-start(bf16[8,1280,128]{2,1,0:T(8,128)(2,1)} %param.8) | copy-start | bytes 7864324
where the time goes:
time: 160 us; the launch traced here: 159 us
  matrix products  58.1 us (36%)
  waiting for transfers between devices  40.7 us (25%)
  starting transfers between devices  24.5 us (15%)
  other arithmetic  11.4 us (7%)
  blocking collectives  10.3 us (6%)
  local copies, waits for them, and re-layouts  9.19 us (6%)
  between operations  4.79 us (3%)
    ppermute x8, waiting for transfers between devices, shift(): return lax.ppermute(value, axis, pairs)  40.7 us
    ppermute x8, starting transfers between devices, shift(): return lax.ppermute(value, axis, pairs)  24.5 us
    psum x1, blocking collectives, on_device(): total_sums = lax.psum(local_sums, ('sub', 'head'))  10.3 us
    dot_general x1, matrix products, on_device(): jnp.einsum('hnij,hnid->hnjd', block_probs, output_grad_blocks, preferred_...  7.37 us
    dot_general x1, matrix products, on_device(): jnp.einsum('bc,hcde->hbde', earlier_mask, key_value_block, precision=high...  7.22 us
    dot_general x1, matrix products, on_device(): jnp.einsum('c,hcde->hde', first_match, query_grad_block, precision=highes...  5.18 us
    dot_general x1, matrix products, on_device(): jnp.einsum('c,hcde->hde', last_match, key_value_block, precision=highest_...  4.89 us
    dot_general x1, local copies, waits for them, and re-layouts, on_device(): jnp.einsum('hnid,hnie->hnde', query_blocks, output_grad_blocks, preferred...  4.7 us
  transfers between devices with their start and end apart: 8, of which 3 were waited for; matrix products, arithmetic and copies ran while one was open for 22% of the time, Pallas kernels for 0%

commit v1 on v0

--- a/solution.py
+++ b/solution.py
@@ -86,7 +86,7 @@
     local_sums = jnp.stack(
         [jnp.sum(raw_attn * raw_attn, axis=(0, 2)), jnp.sum(scaled * raw_attn, axis=(0, 2))]
     )
-    total_sums = lax.psum(local_sums, ("sub", "head"))
+    total_sums = lax.psum(lax.psum(local_sums, "head"), "sub")
     root_mean = jnp.sqrt(total_sums[0] / feature_count + 1e-06)
     inner_mean = total_sums[1] / feature_count
     factor = inner_mean / (root_mean * root_mean)

time: 160 us -> 158 us (0.988)
  waiting for transfers between devices: 40.7 us -> 37.6 us
  blocking collectives: 10.3 us -> 12 us
    ppermute x8, waiting for transfers between devices: 40.7 us -> 37.6 us  [shift(): return lax.ppermute(value, axis, pairs)]
    psum x1 -> x2, blocking collectives: 10.3 us -> 12 us  [on_device(): total_sums = lax.psum(lax.psum(local_sums, 'head'), 'sub')]
where the time goes in v1:
time: 158 us
  matrix products  58.1 us (37%)
  waiting for transfers between devices  37.6 us (24%)
  starting transfers between devices  24.5 us (16%)
  blocking collectives  12 us (8%)
  other arithmetic  11.4 us (7%)
  local copies, waits for them, and re-layouts  9.18 us (6%)
  between operations  4.72 us (3%)
    ppermute x8, waiting for transfers between devices, shift(): return lax.ppermute(value, axis, pairs)  37.6 us
    ppermute x8, starting transfers between devices, shift(): return lax.ppermute(value, axis, pairs)  24.5 us
    psum x2, blocking collectives, on_device(): total_sums = lax.psum(lax.psum(local_sums, 'head'), 'sub')  12 us
    dot_general x1, matrix products, on_device(): jnp.einsum('hnij,hnid->hnjd', block_probs, output_grad_blocks, preferred_...  7.37 us
    dot_general x1, matrix products, on_device(): jnp.einsum('bc,hcde->hbde', earlier_mask, key_value_block, precision=high...  7.21 us
    dot_general x1, matrix products, on_device(): jnp.einsum('c,hcde->hde', first_match, query_grad_block, precision=highes...  5.19 us
    dot_general x1, matrix products, on_device(): jnp.einsum('c,hcde->hde', last_match, key_value_block, precision=highest_...  4.89 us
    dot_general x1, local copies, waits for them, and re-layouts, on_device(): jnp.einsum('hnid,hnie->hnde', query_blocks, output_grad_blocks, preferred...  4.68 us
  transfers between devices with their start and end apart: 8, of which 3 were waited for; matrix products, arithmetic and copies ran while one was open for 22% of the time, Pallas kernels for 0%

profile of v1, /device:TPU:0, one launch (start us, length us, event | category | flops | bytes accessed | tf_op | source)
XLA Modules:
  0.0 157.5 jit_solution(15554806018053834539)
XLA Ops:
  0.6 0.0 copy-start
  0.6 0.8 convert_element_type.63
  1.5 0.6 fusion.34
  2.0 1.3 collective-permute-start.6
  3.3 1.3 collective-permute-start.4
  4.6 7.6 %collective-permute-start.2 = (f32[]{:T(128)}, f32[]{:T(128)}, u32[]{:S(2)}, u32[]{:S(2)}) collective-permute-start(f32[]{:T(128)} %bitcast.7), channel_id=1, source_target_pairs={{0,8},{4,12},{1,9},{5,13},{2,10},{6,14},{3,11},{7,15},{16,24},{20,... | collective-permute-start | bytes 20 | tf_op jit(solution)/shard_map/ppermute | solution.py:17
  12.2 4.9 %collective-permute-start = (f32[]{:T(128)}, f32[]{:T(128)}, u32[]{:S(2)}, u32[]{:S(2)}) collective-permute-start(f32[]{:T(128)} %bitcast.7), channel_id=1, source_target_pairs={{0,4},{4,8},{8,12},{1,5},{5,9},{9,13},{2,6},{6,10},{10,14},{3,7},{... | collective-permute-start | bytes 20 | tf_op jit(solution)/shard_map/ppermute | solution.py:17
  17.1 3.4 %fusion.36 = f32[8,5,128,128]{3,2,1,0:T(8,128)S(1)} fusion(bf16[8,5,256,128]{3,2,1,0:T(8,128)(2,1)} %bitcast.105, bf16[8,5,256,128]{3,2,1,0:T(8,128)(2,1)} %bitcast.109), kind=kOutput, calls=%fused_computation.62 | convolution fusion | flops 335544320 | bytes 7864320 | tf_op jit(solution)/shard_map/hnid,hnie->hnde/dot_general | solution.py:61
  20.5 0.0 copy-start.2
  20.5 1.5 copy-done.2
  22.0 4.9 %fusion.6 = f32[1,8,128,128]{3,0,2,1:T(1,128)} fusion(f32[8,5,128,128]{3,2,1,0:T(8,128)S(1)} %fusion.36, f32[]{:T(128)} %bitcast.7, s32[5]{0:T(128)S(1)} %copy-done.16), kind=kOutput, calls=%fused_computation.16 | convolution fusion | flops 7864330 | bytes 3145752 | tf_op jit(solution)/shard_map/c,hcde->hde/dot_general | solution.py:65
  26.9 1.4 collective-permute-start.1
  28.4 0.0 copy-start.9
  28.4 3.4 %select_convert_fusion.1 = bf16[8,5,256,256]{3,2,1,0:T(8,128)(2,1)S(1)} fusion(pred[256,256]{1,0:T(8,128)(4,1)S(1)} %iota_compare_fusion, bf16[8,5,256,128]{3,2,1,0:T(8,128)(2,1)S(1)} %bitcast.95, bf16[8,5,256,128]{3,2,1,0:T(8,128)(2,1)} %bitcast.106), kind=kOutput, calls=%fused_computation.1 | convolution fusion | flops 676331520 | bytes 10551296 | tf_op jit(solution)/shard_map/hnid,hnjd->hnij/dot_general | solution.py:67
  31.9 0.0 copy-done.9
  31.9 0.0 copy-start.6
  31.9 4.0 %fusion.35 = f32[8,5,256,128]{3,2,1,0:T(8,128)} fusion(bf16[8,5,256,256]{3,2,1,0:T(8,128)(2,1)S(1)} %select_convert_fusion.1, bf16[8,5,256,128]{3,2,1,0:T(8,128)(2,1)S(1)} %bitcast.110), kind=kOutput, calls=%fused_computation.61 | convolution fusion | flops 671088640 | bytes 13107200 | tf_op jit(solution)/shard_map/hnij,hnjd->hnid/dot_general | solution.py:71
  35.9 0.0 collective-permute-done
  37.1 2.2 %collective-permute-done.1 = f32[8,128,128]{2,1,0:T(8,128)S(1)} collective-permute-done((f32[8,128,128]{2,1,0:T(8,128)}, f32[8,128,128]{2,1,0:T(8,128)S(1)}, u32[]{:S(2)}, u32[]{:S(2)}) %collective-permute-start.1) | collective-permute-done | bytes 524320 | tf_op jit(solution)/shard_map/ppermute | solution.py:17
  39.3 1.9 %multiply_add_fusion.3 = f32[8,128,128]{2,1,0:T(8,128)} fusion(f32[8,128,128]{2,1,0:T(8,128)} %bitcast.11, f32[8,128,128]{2,1,0:T(8,128)S(1)} %collective-permute-done.1, f32[]{:T(128)S(6)} %convert_element_type.66, pred[]{:T(512)S(6)} %ge.12), kind=kLoop, calls=%fused_computation.28 | loop fusion | flops 393216 | bytes 1572869 | tf_op jit(solution)/shard_map/add | solution.py:21
  41.2 4.8 %collective-permute-start.3 = (f32[8,128,128]{2,1,0:T(8,128)}, f32[8,128,128]{2,1,0:T(8,128)}, u32[]{:S(2)}, u32[]{:S(2)}) collective-permute-start(f32[8,128,128]{2,1,0:T(8,128)} %multiply_add_fusion.3), channel_id=1, source_target_pairs={{0,8},{4,12},{1,9},{5,13},{2,10},{6,14},{3,11},{7,15},{16,24},{20,... | collective-permute-start | bytes 1572872 | tf_op jit(solution)/shard_map/ppermute | solution.py:17
  46.0 7.2 %fusion.8 = f32[8,128,128,5]{2,3,1,0:T(8,128)} fusion(f32[8,5,128,128]{3,2,1,0:T(8,128)} %copy-done.2, f32[5]{0:T(128)S(1)} %convert_element_type.63), kind=kOutput, calls=%fused_computation.18 | convolution fusion | flops 39321676 | bytes 5242900 | tf_op jit(solution)/shard_map/bc,hcde->hbde/dot_general | solution.py:74
  53.2 0.0 collective-permute-done.4
  54.4 0.0 collective-permute-done.6
  55.1 0.0 collective-permute-done.2
  55.6 0.0 collective-permute-done.3
  55.7 0.1 multiply_add_fusion.2
  55.8 0.0 copy-start.7
  55.8 3.0 %fusion.11 = bf16[8,5,128,128]{3,2,1,0:T(8,128)(2,1)S(1)} fusion(f32[8,128,128,5]{2,3,1,0:T(8,128)} %fusion.8, f32[8,128,128]{2,1,0:T(8,128)S(1)} %multiply_add_fusion.2, f32[5]{0:T(128)S(1)} %get-tuple-element.6), kind=kLoop, calls=%fused_computation.23 | loop fusion | flops 1966080 | bytes 4456468 | tf_op jit(solution)/shard_map/convert_element_type | solution.py:79
  58.7 0.8 copy-done.7
  59.5 1.2 multiply_reduce_fusion
  60.7 1.1 copy-done.14
  61.8 0.8 fusion.2
  62.6 0.5 copy-done.1
  63.1 3.3 %psum.14 = f32[2,1280]{1,0:T(2,128)S(1)} all-reduce(f32[2,1280]{1,0:T(2,128)S(1)} %pad_maximum_fusion), channel_id=1, replica_groups=mesh['groups'=2,'ctx'=4,'sub'=2,'head'=2] {'head'}, use_global_device_ids=true, to_apply=%region_2.3 | all-reduce | flops 2560 | bytes 20480 | tf_op jit(solution)/shard_map/psum | solution.py:89
  66.4 8.7 %psum.15 = f32[2,1280]{1,0:T(2,128)S(1)} all-reduce(f32[2,1280]{1,0:T(2,128)S(1)} %psum.14), channel_id=1, replica_groups=mesh['groups'=2,'ctx'=4,'sub'=2,'head'=2] {'sub'}, use_global_device_ids=true, to_apply=%region_3.4 | all-reduce | flops 2560 | bytes 20480 | tf_op jit(solution)/shard_map/psum | solution.py:89
  75.2 4.0 %fusion.5 = bf16[8,1280,128]{2,1,0:T(8,128)(2,1)S(1)} fusion(f32[8,5,256,128]{3,2,1,0:T(8,128)} %copy-done.1, bf16[8,1280,128]{2,1,0:T(8,128)(2,1)} %param.9, f32[1280]{0:T(1024)S(1)} %get-tuple-element.4, f32[1280]{0:T(1024)S(1)} %multiply_divide_fusion, f32[8,128]{1,0:T(8,128)S(1)} %copy-done.15), kind=kLoop, calls=%fused_computation.11 | loop fusion | flops 7864320 | bytes 10500096 | tf_op jit(solution)/shard_map/convert_element_type | solution.py:93
  79.2 0.0 copy-start.3
  79.2 7.4 %fusion.39 = f32[8,5,256,128]{3,2,1,0:T(8,128)} fusion(bf16[8,5,256,256]{3,2,1,0:T(8,128)(2,1)} %copy-done.6, bf16[8,5,256,128]{3,2,1,0:T(8,128)(2,1)S(1)} %bitcast.99), kind=kOutput, calls=%fused_computation.65 | convolution fusion | flops 671088640 | bytes 13107200 | tf_op jit(solution)/shard_map/hnij,hnid->hnjd/dot_general | solution.py:115
  86.6 2.4 %convolution_bitcast_fusion = f32[8,5,128,128]{2,3,1,0:T(8,128)} fusion(bf16[8,5,256,128]{3,2,1,0:T(8,128)(2,1)S(1)} %bitcast.100, bf16[8,5,256,128]{3,2,1,0:T(8,128)(2,1)S(1)} %bitcast.98), kind=kOutput, calls=%fused_computation.24 | convolution fusion | flops 335544320 | bytes 7864320 | tf_op jit(solution)/shard_map/hnid,hnie->hnde/dot_general | solution.py:97
  89.0 3.8 %select_convert_fusion = bf16[8,5,256,256]{3,2,1,0:T(8,128)(2,1)} fusion(pred[256,256]{1,0:T(8,128)(4,1)S(1)} %iota_compare_fusion, bf16[8,5,256,128]{3,2,1,0:T(8,128)(2,1)S(1)} %bitcast.101, bf16[8,5,256,128]{3,2,1,0:T(8,128)(2,1)S(1)} %bitcast.111), kind=kOutput, calls=%fused_computation | convolution fusion | flops 676331520 | bytes 10551296 | tf_op jit(solution)/shard_map/hnid,hnjd->hnij/dot_general | solution.py:105
  92.8 4.7 %copy.29 = f32[8,5,128,128]{3,1,2,0:T(8,128)} copy(f32[8,5,128,128]{2,3,1,0:T(8,128)} %convolution_bitcast_fusion) | data formatting | bytes 5242880 | tf_op jit(solution)/shard_map/hnid,hnie->hnde/dot_general | solution.py:97
  97.5 5.2 %fusion.25 = f32[1,8,128,128]{3,0,2,1:T(1,128)S(1)} fusion(f32[8,5,128,128]{3,1,2,0:T(8,128)} %copy.29, f32[]{:T(128)} %bitcast.21, s32[5]{0:T(128)S(1)} %copy-done.16), kind=kOutput, calls=%fused_computation.49 | convolution fusion | flops 7864330 | bytes 3145752 | tf_op jit(solution)/shard_map/c,hcde->hde/dot_general | solution.py:101
  102.7 0.0 slice-start.1
  102.7 1.4 collective-permute-start.5
  104.1 0.0 copy-start.8
  104.1 4.2 %fusion.38 = f32[8,5,256,128]{3,2,1,0:T(8,128)S(1)} fusion(bf16[8,5,256,256]{3,2,1,0:T(8,128)(2,1)} %select_convert_fusion, bf16[8,5,256,128]{3,2,1,0:T(8,128)(2,1)S(1)} %bitcast.97), kind=kOutput, calls=%fused_computation.64 | convolution fusion | flops 671088640 | bytes 13107200 | tf_op jit(solution)/shard_map/hnij,hnid->hnjd/dot_general | solution.py:112
  108.4 1.5 fusion.37
  109.9 15.6 %collective-permute-done.5 = f32[8,128,128]{2,1,0:T(8,128)S(1)} collective-permute-done((f32[8,128,128]{2,1,0:T(8,128)S(1)}, f32[8,128,128]{2,1,0:T(8,128)S(1)}, u32[]{:S(2)}, u32[]{:S(2)}) %collective-permute-start.5) | collective-permute-done | bytes 524320 | tf_op jit(solution)/shard_map/ppermute | solution.py:17
  125.5 0.1 multiply_add_fusion.1
  125.6 0.0 copy-start.4
  125.6 0.0 copy-start.13
  125.6 1.8 %collective-permute-start.7 = (f32[8,128,128]{2,1,0:T(8,128)S(1)}, f32[8,128,128]{2,1,0:T(8,128)S(1)}, u32[]{:S(2)}, u32[]{:S(2)}) collective-permute-start(f32[8,128,128]{2,1,0:T(8,128)S(1)} %multiply_add_fusion.1), channel_id=1, source_target_pairs={{8,0},{12,4},{9,1},{13,5},{10,2},{14,6},{11,3},{15,7},{24,16},{28,... | collective-permute-start | bytes 1572872 | tf_op jit(solution)/shard_map/ppermute | solution.py:17
  127.4 0.0 copy-done.5
  127.4 0.0 slice-start.2
  127.4 2.2 %fusion.19 = f32[8,128,128,5]{2,3,1,0:T(8,128)S(1)} fusion(f32[8,5,128,128]{3,1,2,0:T(8,128)S(1)} %copy-done.5, f32[5]{0:T(128)S(1)} %convert_element_type.63), kind=kOutput, calls=%fused_computation.44 | convolution fusion | flops 39321676 | bytes 5242900 | tf_op jit(solution)/shard_map/bc,hcde->hbde/dot_general | solution.py:118
  129.7 0.0 slice-start.3
  129.7 2.4 %add_convert_fusion = bf16[8,5,256,128]{3,2,1,0:T(8,128)(2,1)} fusion(f32[8,5,256,128]{3,2,1,0:T(8,128)S(1)} %fusion.37, bf16[8,5,256,128]{3,2,1,0:T(8,128)(2,1)S(1)} %bitcast.102, bf16[8,5,128,128]{3,2,1,0:T(8,128)(2,1)S(1)} %copy-done.13), kind=kOutput, calls=%fused_computation.13 | convolution fusion | flops 338165760 | bytes 11796480 | tf_op jit(solution)/shard_map/hnie,hnde->hnid/dot_general | solution.py:124
  132.1 19.8 %collective-permute-done.7 = f32[8,128,128]{2,1,0:T(8,128)S(1)} collective-permute-done((f32[8,128,128]{2,1,0:T(8,128)S(1)}, f32[8,128,128]{2,1,0:T(8,128)S(1)}, u32[]{:S(2)}, u32[]{:S(2)}) %collective-permute-start.7) | collective-permute-done | bytes 524320 | tf_op jit(solution)/shard_map/ppermute | solution.py:17
  151.9 0.1 multiply_add_fusion
  152.0 0.6 fusion.10
  152.7 0.0 copy-start.11
  152.7 2.4 %fusion = bf16[8,5,256,128]{3,2,1,0:T(8,128)(2,1)} fusion(f32[8,5,256,128]{3,2,1,0:T(8,128)S(1)} %bitcast.114, bf16[8,5,256,128]{3,2,1,0:T(8,128)(2,1)S(1)} %bitcast.108, bf16[8,5,128,128]{3,2,1,0:T(8,128)(2,1)S(1)} %fusion.10), kind=kOutput, calls=%fused_computation.3 | convolution fusion | flops 338165760 | bytes 11796480 | tf_op jit(solution)/shard_map/hnid,hnde->hnie/dot_general | solution.py:130
  155.1 2.4 %fusion.1 = bf16[8,5,256,128]{3,2,1,0:T(8,128)(2,1)} fusion(f32[8,5,256,128]{3,2,1,0:T(8,128)S(1)} %fusion.38, bf16[8,5,128,128]{3,2,1,0:T(8,128)(2,1)S(1)} %fusion.10, bf16[8,5,256,128]{3,2,1,0:T(8,128)(2,1)S(1)} %bitcast.112), kind=kOutput, calls=%fused_computation.5 | convolution fusion | flops 338165760 | bytes 11796480 | tf_op jit(solution)/shard_map/hnie,hnde->hnid/dot_general | solution.py:127
  (32 shorter events, 0.2 us)
Async XLA Ops:
  0.6 27.8 %copy-start = (bf16[8,1280,128]{2,1,0:T(8,128)(2,1)S(1)}, bf16[8,1280,128]{2,1,0:T(8,128)(2,1)}, u32[]{:S(2)}) copy-start(bf16[8,1280,128]{2,1,0:T(8,128)(2,1)} %param.6) | copy-start | bytes 7864324
  2.0 52.4 %collective-permute-start.6 = (f32[]{:T(128)}, f32[]{:T(128)}, u32[]{:S(2)}, u32[]{:S(2)}) collective-permute-start(f32[]{:T(128)} %bitcast.21), channel_id=1, source_target_pairs={{8,0},{12,4},{9,1},{13,5},{10,2},{14,6},{11,3},{15,7},{24,16},{28,... | collective-permute-start | bytes 20 | tf_op jit(solution)/shard_map/ppermute | solution.py:17
  3.3 49.8 %collective-permute-start.4 = (f32[]{:T(128)}, f32[]{:T(128)}, u32[]{:S(2)}, u32[]{:S(2)}) collective-permute-start(f32[]{:T(128)} %bitcast.21), channel_id=1, source_target_pairs={{4,0},{8,4},{12,8},{5,1},{9,5},{13,9},{6,2},{10,6},{14,10},{7,3},{... | collective-permute-start | bytes 20 | tf_op jit(solution)/shard_map/ppermute | solution.py:17
  4.6 50.4 %collective-permute-start.2 = (f32[]{:T(128)}, f32[]{:T(128)}, u32[]{:S(2)}, u32[]{:S(2)}) collective-permute-start(f32[]{:T(128)} %bitcast.7), channel_id=1, source_target_pairs={{0,8},{4,12},{1,9},{5,13},{2,10},{6,14},{3,11},{7,15},{16,24},{20,... | collective-permute-start | bytes 20 | tf_op jit(solution)/shard_map/ppermute | solution.py:17
  12.2 23.7 %collective-permute-start = (f32[]{:T(128)}, f32[]{:T(128)}, u32[]{:S(2)}, u32[]{:S(2)}) collective-permute-start(f32[]{:T(128)} %bitcast.7), channel_id=1, source_target_pairs={{0,4},{4,8},{8,12},{1,5},{5,9},{9,13},{2,6},{6,10},{10,14},{3,7},{... | collective-permute-start | bytes 20 | tf_op jit(solution)/shard_map/ppermute | solution.py:17
  17.1 4.9 %copy-start.16 = (s32[5]{0:T(128)S(1)}, s32[5]{0:T(128)}, u32[]{:S(2)}) copy-start(s32[5]{0:T(128)} %param.11) | copy-start | bytes 64
  20.5 1.5 copy-start.2
  26.9 12.3 %collective-permute-start.1 = (f32[8,128,128]{2,1,0:T(8,128)}, f32[8,128,128]{2,1,0:T(8,128)S(1)}, u32[]{:S(2)}, u32[]{:S(2)}) collective-permute-start(f32[8,128,128]{2,1,0:T(8,128)} %bitcast.11), channel_id=1, source_target_pairs={{0,4},{4,8},{8,12},{1,5},{5,9},{9,13},{2,6},{6,10},{10,14},{3,7},{... | collective-permute-start | bytes 1572872 | tf_op jit(solution)/shard_map/ppermute | solution.py:17
  28.4 3.4 %copy-start.9 = (bf16[8,1280,128]{2,1,0:T(8,128)(2,1)S(1)}, bf16[8,1280,128]{2,1,0:T(8,128)(2,1)}, u32[]{:S(2)}) copy-start(bf16[8,1280,128]{2,1,0:T(8,128)(2,1)} %param.8) | copy-start | bytes 7864324
  31.9 4.0 %copy-start.6 = (bf16[8,5,256,256]{3,2,1,0:T(8,128)(2,1)}, bf16[8,5,256,256]{3,2,1,0:T(8,128)(2,1)S(1)}, u32[]{:S(2)}) copy-start(bf16[8,5,256,256]{3,2,1,0:T(8,128)(2,1)S(1)} %select_convert_fusion.1) | copy-start | bytes 15728644
  41.2 14.5 %collective-permute-start.3 = (f32[8,128,128]{2,1,0:T(8,128)}, f32[8,128,128]{2,1,0:T(8,128)}, u32[]{:S(2)}, u32[]{:S(2)}) collective-permute-start(f32[8,128,128]{2,1,0:T(8,128)} %multiply_add_fusion.3), channel_id=1, source_target_pairs={{0,8},{4,12},{1,9},{5,13},{2,10},{6,14},{3,11},{7,15},{16,24},{20,... | collective-permute-start | bytes 1572872 | tf_op jit(solution)/shard_map/ppermute | solution.py:17
  55.8 3.7 %copy-start.7 = (f32[8,5,256,128]{3,2,1,0:T(8,128)S(1)}, f32[8,5,256,128]{3,2,1,0:T(8,128)}, u32[]{:S(2)}) copy-start(f32[8,5,256,128]{3,2,1,0:T(8,128)} %fusion.35) | copy-start | bytes 15728644
  59.5 1.2 copy-start.12
  59.5 2.3 %copy-start.14 = (bf16[8,1280,128]{2,1,0:T(8,128)(2,1)S(1)}, bf16[8,1280,128]{2,1,0:T(8,128)(2,1)}, u32[]{:S(2)}) copy-start(bf16[8,1280,128]{2,1,0:T(8,128)(2,1)} %param.9) | copy-start | bytes 7864324
  59.5 2.3 %copy-start.15 = (f32[8,128]{1,0:T(8,128)S(1)}, f32[8,128]{1,0:T(8,128)}, u32[]{:S(2)}) copy-start(f32[8,128]{1,0:T(8,128)} %param.10) | copy-start | bytes 12292
  60.7 2.4 %copy-start.1 = (f32[8,5,256,128]{3,2,1,0:T(8,128)}, f32[8,5,256,128]{3,2,1,0:T(8,128)S(1)}, u32[]{:S(2)}) copy-start(f32[8,5,256,128]{3,2,1,0:T(8,128)S(1)} %get-tuple-element.10) | copy-start | bytes 15728644
  79.2 9.8 %copy-start.3 = (bf16[8,1280,128]{2,1,0:T(8,128)(2,1)}, bf16[8,1280,128]{2,1,0:T(8,128)(2,1)S(1)}, u32[]{:S(2)}) copy-start(bf16[8,1280,128]{2,1,0:T(8,128)(2,1)S(1)} %fusion.5) | copy-start | bytes 7864324
  86.6 2.4 %copy-start.10 = (bf16[8,1280,128]{2,1,0:T(8,128)(2,1)S(1)}, bf16[8,1280,128]{2,1,0:T(8,128)(2,1)}, u32[]{:S(2)}) copy-start(bf16[8,1280,128]{2,1,0:T(8,128)(2,1)} %param.8) | copy-start | bytes 7864324
  97.5 10.9 %slice-start = ((s8[5242880]{0:T(1024)(128)(4,1)}), s8[4194304]{0:T(1024)(128)(4,1)S(1)}, s32[]{:S(2)}) async-start(s8[5242880]{0:T(1024)(128)(4,1)} %bitcast.103), calls=%async_computation | async-start | bytes 8388608
  102.7 5.7 %slice-start.1 = ((s8[5242880]{0:T(1024)(128)(4,1)}), s8[1048576]{0:T(1024)(128)(4,1)S(1)}, s32[]{:S(2)}) async-start(s8[5242880]{0:T(1024)(128)(4,1)} %bitcast.103), calls=%async_computation.1 | async-start | bytes 2097152
  102.7 22.8 %collective-permute-start.5 = (f32[8,128,128]{2,1,0:T(8,128)S(1)}, f32[8,128,128]{2,1,0:T(8,128)S(1)}, u32[]{:S(2)}, u32[]{:S(2)}) collective-permute-start(f32[8,128,128]{2,1,0:T(8,128)S(1)} %bitcast.118), channel_id=1, source_target_pairs={{4,0},{8,4},{12,8},{5,1},{9,5},{13,9},{6,2},{10,6},{14,10},{7,3},{... | collective-permute-start | bytes 1572872 | tf_op jit(solution)/shard_map/ppermute | solution.py:17
  104.1 4.2 %copy-start.8 = (bf16[8,1280,128]{2,1,0:T(8,128)(2,1)S(1)}, bf16[8,1280,128]{2,1,0:T(8,128)(2,1)}, u32[]{:S(2)}) copy-start(bf16[8,1280,128]{2,1,0:T(8,128)(2,1)} %param.7) | copy-start | bytes 7864324
  108.4 19.0 %copy-start.5 = (f32[8,5,128,128]{3,1,2,0:T(8,128)S(1)}, f32[8,5,128,128]{3,1,2,0:T(8,128)}, u32[]{:S(2)}) copy-start(f32[8,5,128,128]{3,1,2,0:T(8,128)} %copy.29) | copy-start | bytes 7864324
  125.6 4.1 %copy-start.4 = (bf16[8,1280,128]{2,1,0:T(8,128)(2,1)S(1)}, bf16[8,1280,128]{2,1,0:T(8,128)(2,1)}, u32[]{:S(2)}) copy-start(bf16[8,1280,128]{2,1,0:T(8,128)(2,1)} %copy-done.3) | copy-start | bytes 7864324
  125.6 4.1 %copy-start.13 = (bf16[8,5,128,128]{3,2,1,0:T(8,128)(2,1)S(1)}, bf16[8,5,128,128]{3,2,1,0:T(8,128)(2,1)}, u32[]{:S(2)}) copy-start(bf16[8,5,128,128]{3,2,1,0:T(8,128)(2,1)} %copy-done.12) | copy-start | bytes 3932164
  125.6 26.3 %collective-permute-start.7 = (f32[8,128,128]{2,1,0:T(8,128)S(1)}, f32[8,128,128]{2,1,0:T(8,128)S(1)}, u32[]{:S(2)}, u32[]{:S(2)}) collective-permute-start(f32[8,128,128]{2,1,0:T(8,128)S(1)} %multiply_add_fusion.1), channel_id=1, source_target_pairs={{8,0},{12,4},{9,1},{13,5},{10,2},{14,6},{11,3},{15,7},{24,16},{28,... | collective-permute-start | bytes 1572872 | tf_op jit(solution)/shard_map/ppermute | solution.py:17
  127.4 25.2 %slice-start.2 = ((s8[5242880]{0:T(1024)(128)(4,1)}), s8[4194304]{0:T(1024)(128)(4,1)S(1)}, s32[]{:S(2)}) async-start(s8[5242880]{0:T(1024)(128)(4,1)} %bitcast.113), calls=%async_computation.2 | async-start | bytes 8388608
  129.7 23.0 %slice-start.3 = ((s8[5242880]{0:T(1024)(128)(4,1)}), s8[1048576]{0:T(1024)(128)(4,1)S(1)}, s32[]{:S(2)}) async-start(s8[5242880]{0:T(1024)(128)(4,1)} %bitcast.113), calls=%async_computation.3 | async-start | bytes 2097152
  152.7 2.4 %copy-start.11 = (bf16[8,1280,128]{2,1,0:T(8,128)(2,1)S(1)}, bf16[8,1280,128]{2,1,0:T(8,128)(2,1)}, u32[]{:S(2)}) copy-start(bf16[8,1280,128]{2,1,0:T(8,128)(2,1)} %param.8) | copy-start | bytes 7864324
